TPU v7x, 32 devices: a whole 2x2x4 slice. The times are simulated.
32 devices in a mesh: ctx: 8 (over z, y), ch: 4 (over x, core).
Axes of the slice: x: 2, y: 2, z: 4, core: 2. Of those that a mesh axis runs over, the one named last changes fastest.
Arguments:
- projected: bfloat16 [3, 8192, 4096], P(None, 'ctx', 'ch'), may hold values from -6 to 6
- tap_weights: bfloat16 [3, 3, 4096], P(None, None, 'ch'), may hold values from -3.59375 to 3.59375
- pole_rates: float32 [16, 4096], P(None, 'ch'), may hold values from 1.2207031e-05 to 0.0625
- residues: float32 [16, 4096], P(None, 'ch'), may hold values from -1.4143862 to 1.4143862
- long_bias: float32 [4096], P('ch'), may hold values from -4 to 4
- out_weight: bfloat16 [4096, 4096], P(None, 'ch'), may hold values from -0.09375 to 0.09375
Outputs:
- mixed_out: bfloat16 [8192, 4096], P('ctx', 'ch')
All inputs are finite; a program needn't handle non-finite values.
Results may differ from a plain program's by a relative error of at most 0.012.
Values may be sent and summed in bfloat16 or wider, within the bound.
No kernel may reach another device: no remote copies, remote signals or barrier semaphores. Data moves between devices by JAX's collectives and lax.ppermute only.
A program may use at most 256 MiB of HBM per device.

v0:
```python
import jax
import jax.numpy as jnp
from jax import lax
from jax.sharding import PartitionSpec as P

BLOCK = 64


def shifted(value, axis, steps):
    count = lax.axis_size(axis)
    initial, last = (max(0, -steps), min(count, count - steps))
    return lax.ppermute(value, axis, [(source, source + steps) for source in range(initial, last)])


def make_tables(pole_rates, residues, block_size):
    lag_steps = jnp.arange(block_size, dtype=jnp.float32)
    powers = jnp.exp(-pole_rates[None, :, :] * lag_steps[:, None, None])
    kernel = jnp.sum(powers * residues[None, :, :], axis=1)
    offsets = (
        jnp.arange(block_size, dtype=jnp.int32)[:, None]
        - jnp.arange(block_size, dtype=jnp.int32)[None, :]
    )
    toeplitz = jnp.where(
        (offsets >= 0)[:, :, None], kernel[jnp.maximum(offsets, 0)], jnp.float32(0.0)
    )
    end_weights = powers[::-1]
    read_weights = powers * jnp.exp(-pole_rates)[None, :, :] * residues[None, :, :]
    block_decay = jnp.exp(-pole_rates * block_size)
    return (toeplitz, end_weights, read_weights, block_decay)


def combine(earlier, latter):
    return (earlier[0] * latter[0], latter[0] * earlier[1] + latter[1])


def channel_conv(rows_last, pole_rates, residues):
    highest = lax.Precision.HIGHEST
    channel_count = rows_last.shape[0]
    length = rows_last.shape[1]
    block_count = length // BLOCK
    pole_count = pole_rates.shape[0]
    toeplitz, end_weights, read_weights, block_decay = make_tables(pole_rates, residues, BLOCK)
    toeplitz_c = jnp.transpose(toeplitz, (2, 0, 1))
    blocks = rows_last.astype(jnp.float32).reshape(channel_count, block_count, BLOCK)
    inner_part = jnp.einsum("cij,cnj->cni", toeplitz_c, blocks, precision=highest)
    closing = jnp.einsum("jpc,cnj->ncp", end_weights, blocks, precision=highest)
    closing = closing.reshape(block_count, channel_count * pole_count)
    decay_row = jnp.transpose(block_decay).reshape(1, channel_count * pole_count)
    decays = jnp.broadcast_to(decay_row, closing.shape)
    _, states = lax.associative_scan(combine, (decays, closing), axis=0)
    before_state = jnp.concatenate([jnp.zeros_like(states[:1]), states[:-1]], 0)
    before_state = before_state.reshape(block_count, channel_count, pole_count)
    carried = jnp.einsum("ipc,ncp->cni", read_weights, before_state, precision=highest)
    return (inner_part + carried).reshape(channel_count, length)


def shards(projected, tap_weights, pole_rates, residues, long_bias, out_weight):
    row_count = projected.shape[1]
    rim_rows = tap_weights.shape[0] - 1
    prior_rows = shifted(projected[:, row_count - rim_rows :], "ctx", 1)
    extended = jnp.concatenate([prior_rows, projected], 1)
    featured = jnp.zeros(projected.shape, jnp.float32)
    for tap_index in range(rim_rows + 1):
        lead_row = rim_rows - tap_index
        featured = featured + tap_weights[tap_index].astype(jnp.float32)[:, None, :] * extended[
            :, lead_row : lead_row + row_count
        ].astype(jnp.float32)
    mixed_input = (featured[1] * featured[2]).astype(jnp.bfloat16)
    channel_major = jnp.transpose(mixed_input)
    spread = lax.all_to_all(channel_major, "ctx", split_axis=0, concat_axis=1, tiled=True)
    share_width = spread.shape[0]
    first_channel = lax.axis_index("ctx") * share_width
    rates_here = lax.dynamic_slice_in_dim(pole_rates, first_channel, share_width, 1)
    residues_here = lax.dynamic_slice_in_dim(residues, first_channel, share_width, 1)
    long_part = channel_conv(spread, rates_here, residues_here).astype(jnp.bfloat16)
    returned = lax.all_to_all(long_part, "ctx", split_axis=1, concat_axis=0, tiled=True)
    long_mix = jnp.transpose(returned)
    gated_mix = featured[0] * (
        long_mix.astype(jnp.float32) + long_bias[None, :] * mixed_input.astype(jnp.float32)
    )
    gated_mix = gated_mix.astype(jnp.bfloat16)
    mixed_out = jnp.dot(
        lax.all_gather(gated_mix, "ch", axis=1, tiled=True),
        out_weight,
        preferred_element_type=jnp.float32,
    )
    return mixed_out.astype(jnp.bfloat16)


def solution(mesh):
    in_specs = (
        P(None, "ctx", "ch"),
        P(None, None, "ch"),
        P(None, "ch"),
        P(None, "ch"),
        P("ch"),
        P(None, "ch"),
    )
    out_specs = P("ctx", "ch")
    return jax.shard_map(shards, mesh=mesh, in_specs=in_specs, out_specs=out_specs, check_vma=False)
```

profile of v0, /device:TPU:0, one launch (start us, length us, event | category | flops | bytes accessed | tf_op | source)
XLA Modules:
  0.0 405.2 jit_solution(4329657434524788336)
XLA Ops:
  7.4 4.9 %collective-permute-start = (bf16[3,2,1024]{2,1,0:T(2,128)(2,1)S(1)}, bf16[3,2,1024]{2,1,0:T(2,128)(2,1)S(1)}, u32[]{:S(2)}, u32[]{:S(2)}) collective-permute-start(bf16[3,2,1024]{2,1,0:T(2,128)(2,1)S(1)} %slice.176), channel_id=1, source_target_pairs={{0,4},{4,8},{8,12},{12,16},{16,20},{20,24},{24,28},{1,5},{5,9},{9,... | collective-permute-start | bytes 36872 | tf_op jit(solution)/shard_map/ppermute | solution.py:12
  13.0 8.7 %copy.43 = bf16[3,1024,1024]{1,2,0:T(8,128)(2,1)} copy(bf16[3,1024,1024]{2,1,0:T(8,128)(2,1)} %param.6) | data formatting | bytes 12582912 | tf_op args[0]
  22.1 15.7 %multiply_add_fusion = f32[3,1024,1024]{1,2,0:T(8,128)S(1)} fusion(bf16[3,1024,1024]{1,2,0:T(8,128)(2,1)} %copy.43, bf16[3,2,1024]{1,2,0:T(8,128)(2,1)S(1)} %copy.44, f32[3,1024]{1,0:T(4,128)S(1)} %get-tuple-element.12, f32[3,1024]{1,0:T(4,128)S(1)} %get-tuple-element.13, f32[3,1024]{1,0:T(4,128)S(1)} %get-tuple-element.11), kind=kLoop, calls=%fused_computation.1 | loop fusion | flops 44040192 | bytes 18923520 | tf_op jit(solution)/shard_map/add | solution.py:65
  37.8 4.5 %copy-done = f32[3,1024,1024]{1,2,0:T(8,128)} copy-done((f32[3,1024,1024]{1,2,0:T(8,128)}, f32[3,1024,1024]{1,2,0:T(8,128)S(1)}, u32[]{:S(2)}) %copy-start) | copy-done | bytes 12582936
  44.3 4.9 %all-to-all-start = ((bf16[8,128,1024]{2,1,0:T(8,128)(2,1)}), bf16[8,128,1024]{2,1,0:T(8,128)(2,1)}, u32[]{:S(2)}, u32[]{:S(2)}) async-start(bf16[8,128,1024]{2,1,0:T(8,128)(2,1)} %bitcast.6), calls=%async_computation | async-start | bytes 4194304 | tf_op jit(solution)/shard_map/all_to_all | solution.py:70
  53.5 10.8 %gather_fusion = f32[4096,128]{1,0:T(8,128)S(1)} fusion(f32[64,128]{1,0:T(8,128)S(1)} %copy.49, s32[4096]{0:T(1024)S(1)} %broadcast_clamp_fusion), kind=kCustom, calls=%fused_computation | custom fusion | bytes 4210688 | tf_op jit(solution)/shard_map/gather | solution.py:24
  64.3 4.6 %copy.50 = f32[64,64,128]{1,0,2:T(8,128)} copy(f32[64,64,128]{2,1,0:T(8,128)S(1)} %bitcast.56) | data formatting | bytes 4194304 | tf_op jit(solution)/shard_map/gather | solution.py:24
  70.8 26.5 %all-to-all-done = bf16[8,128,1024]{2,1,0:T(8,128)(2,1)} async-done(((bf16[8,128,1024]{2,1,0:T(8,128)(2,1)}), bf16[8,128,1024]{2,1,0:T(8,128)(2,1)}, u32[]{:S(2)}, u32[]{:S(2)}) %all-to-all-start) | async-done | bytes 2097184 | tf_op jit(solution)/shard_map/all_to_all | solution.py:70
  97.3 3.9 copy.46
  101.2 3.8 copy.51
  105.0 3.0 fusion.25
  108.0 20.3 %slice.187 = f32[64,2048]{0,1:T(8,128)} slice(f32[128,2048]{0,1:T(8,128)S(1)} %bitcast.52), slice={[0:127:2], [0:2048:1]} | slice | bytes 1048576 | tf_op jit(solution)/shard_map/slice | solution.py:50
  128.3 21.9 %slice.188 = f32[64,2048]{0,1:T(8,128)} slice(f32[128,2048]{0,1:T(8,128)S(1)} %bitcast.53), slice={[1:128:2], [0:2048:1]} | slice | bytes 1048576 | tf_op jit(solution)/shard_map/slice | solution.py:50
  184.5 21.6 %slice.226 = f32[63,2048]{0,1:T(8,128)} slice(f32[128,2048]{0,1:T(8,128)S(1)} %bitcast.54), slice={[2:128:2], [0:2048:1]} | slice | bytes 1032192 | tf_op jit(solution)/shard_map/slice | solution.py:50
  220.8 2.7 pad.55
  225.6 4.6 %pad.116 = f32[128,2048]{1,0:T(8,128)} pad(f32[64,2048]{1,0:T(8,128)} %add.128, f32[]{:T(128)} %constant.5.clone.1), padding=1_0_1x0_0_0 | pad | bytes 1572868
  243.5 4.2 %fusion.4 = f32[128,128,64]{1,2,0:T(8,128)S(1)} fusion(bf16[128,128,64]{1,2,0:T(8,128)(2,1)S(1)} %copy.51, f32[64,64,128]{1,0,2:T(8,128)} %copy.50, pred[64,64]{1,0:T(8,128)(4,1)S(1)} %copy-done.8), kind=kOutput, calls=%fused_computation.12 | convolution fusion | flops 805830656 | bytes 8392704 | tf_op jit(solution)/shard_map/cij,cnj->cni/dot_general | solution.py:45
  247.7 7.8 %add_convert_fusion = bf16[128,128,64]{1,2,0:T(8,128)(2,1)S(1)} fusion(f32[128,128,64]{1,2,0:T(8,128)S(1)} %fusion.4, f32[128,128,16]{0,2,1:T(8,128)S(1)} %bitcast.59, f32[16,128]{0,1:T(8,128)S(1)} %copy-done.6, f32[16,128]{0,1:T(8,128)S(1)} %copy-done.5, f32[16,128]{0,1:T(8,128)S(1)} %copy-done.3), kind=kOutput, calls=%fused_computation.15 | convolution fusion | flops 203816960 | bytes 7364608 | tf_op jit(solution)/shard_map/ipc,ncp->cni/dot_general | solution.py:53
  255.6 3.3 copy.60
  258.8 52.0 %all_to_all.26 = bf16[128,8,1024]{0,2,1:T(8,128)(2,1)S(1)} all-to-all(bf16[128,8,1024]{0,2,1:T(8,128)(2,1)} %bitcast.58), channel_id=1, replica_groups=mesh['ctx'=8,'ch'=4] {'ctx'}, dimensions={1} | all-to-all | bytes 4194304 | tf_op jit(solution)/shard_map/all_to_all | solution.py:76
  313.1 5.4 %copy.61 = f32[8,128,1024]{2,1,0:T(8,128)} copy(f32[8,128,1024]{1,2,0:T(8,128)} %convert_bitcast_fusion) | data formatting | bytes 8388608 | tf_op jit(solution)/shard_map/convert_element_type | solution.py:79
  318.5 7.7 %fusion.3 = bf16[1024,1024]{0,1:T(8,128)(2,1)} fusion(f32[3,1024,1024]{1,2,0:T(8,128)} %copy-done, f32[8,128,1024]{2,1,0:T(8,128)} %copy.61, f32[1024]{0:T(1024)S(1)} %copy-done.9), kind=kLoop, calls=%fused_computation.10 | loop fusion | flops 7340032 | bytes 18878464 | tf_op jit(solution)/shard_map/convert_element_type | solution.py:81
  326.2 57.5 %all-gather.2.cloned.1.call-done = bf16[1024,4096]{0,1:T(8,128)(2,1)} async-done(((bf16[1024,1024]{0,1:T(8,128)(2,1)}), bf16[1024,4096]{0,1:T(8,128)(2,1)}) %all-gather.2.cloned.1.call-update) | async-done | bytes 8388624 | tf_op jit(solution)/shard_map/all_gather | solution.py:83
  383.7 14.7 %convolution_convert_fusion = bf16[1024,1024]{1,0:T(8,128)(2,1)} fusion(bf16[1024,4096]{0,1:T(8,128)(2,1)} %all-gather.2.cloned.1.call-done, bf16[4096,1024]{1,0:T(8,128)(2,1)} %param.11), kind=kOutput, calls=%fused_computation.19 | convolution fusion | flops 8590983168 | bytes 18874368 | tf_op jit(solution)/shard_map/dot_general | solution.py:82
  (107 shorter events, 76.7 us)
Async XLA Ops:
  7.4 14.3 %collective-permute-start = (bf16[3,2,1024]{2,1,0:T(2,128)(2,1)S(1)}, bf16[3,2,1024]{2,1,0:T(2,128)(2,1)S(1)}, u32[]{:S(2)}, u32[]{:S(2)}) collective-permute-start(bf16[3,2,1024]{2,1,0:T(2,128)(2,1)S(1)} %slice.176), channel_id=1, source_target_pairs={{0,4},{4,8},{8,12},{12,16},{16,20},{20,24},{24,28},{1,5},{5,9},{9,... | collective-permute-start | bytes 36872 | tf_op jit(solution)/shard_map/ppermute | solution.py:12
  37.8 4.5 %copy-start = (f32[3,1024,1024]{1,2,0:T(8,128)}, f32[3,1024,1024]{1,2,0:T(8,128)S(1)}, u32[]{:S(2)}) copy-start(f32[3,1024,1024]{1,2,0:T(8,128)S(1)} %multiply_add_fusion) | copy-start | bytes 37748740
  44.3 52.9 %all-to-all-start = ((bf16[8,128,1024]{2,1,0:T(8,128)(2,1)}), bf16[8,128,1024]{2,1,0:T(8,128)(2,1)}, u32[]{:S(2)}, u32[]{:S(2)}) async-start(bf16[8,128,1024]{2,1,0:T(8,128)(2,1)} %bitcast.6), calls=%async_computation | async-start | bytes 4194304 | tf_op jit(solution)/shard_map/all_to_all | solution.py:70
  49.2 334.5 %all-gather.2.cloned.1.call-start = ((), (), s32[]{:S(2)}) async-start(), calls=%async_computation.2 | async-start | bytes 10485760 | tf_op jit(solution)/shard_map/all_gather | solution.py:83
  50.1 3.4 copy-start.2
  50.2 3.3 copy-start.4
  70.8 89.6 %copy-start.7 = (f32[2048]{0:T(1024)}, f32[2048]{0:T(1024)S(1)}, u32[]{:S(2)}) copy-start(f32[2048]{0:T(1024)S(1)} %get-tuple-element.17) | copy-start | bytes 24580
  181.4 37.7 %slice-start = ((f32[64,2048]{1,0:T(8,128)}), f32[1,2048]{1,0:T(1,128)S(1)}, s32[]{:S(2)}) async-start(f32[64,2048]{1,0:T(8,128)} %multiply_add_fusion.1), calls=%async_computation.3 | async-start | bytes 16384 | tf_op jit(solution)/shard_map/slice | solution.py:50
  210.8 0.7 copy-start.1
  237.2 6.3 %copy-start.8 = (pred[64,64]{1,0:T(8,128)(4,1)S(1)}, pred[64,64]{1,0:T(8,128)(4,1)}, u32[]{:S(2)}) copy-start(pred[64,64]{1,0:T(8,128)(4,1)} %subtract_compare_fusion) | copy-start | bytes 12292
  243.5 4.2 %copy-start.3 = (f32[16,128]{0,1:T(8,128)S(1)}, f32[16,128]{0,1:T(8,128)}, u32[]{:S(2)}) copy-start(f32[16,128]{0,1:T(8,128)} %copy-done.2) | copy-start | bytes 24580
  243.5 4.2 %copy-start.5 = (f32[16,128]{0,1:T(8,128)S(1)}, f32[16,128]{0,1:T(8,128)}, u32[]{:S(2)}) copy-start(f32[16,128]{0,1:T(8,128)} %copy-done.4) | copy-start | bytes 24580
  243.5 4.2 %copy-start.6 = (f32[16,128]{0,1:T(8,128)S(1)}, f32[16,128]{0,1:T(8,128)}, u32[]{:S(2)}) copy-start(f32[16,128]{0,1:T(8,128)} %copy.59) | copy-start | bytes 24580
  313.1 5.4 %copy-start.9 = (f32[1024]{0:T(1024)S(1)}, f32[1024]{0:T(1024)}, u32[]{:S(2)}) copy-start(f32[1024]{0:T(1024)} %param.10) | copy-start | bytes 12292
Sparse Core Ops, SparseCore 0:
  326.3 57.3 all-gather.1
where the time goes:
time: 408 us; the launch traced here: 405 us
  local copies, waits for them, and re-layouts  157 us (38%)
  waiting for transfers between devices  84 us (21%)
  other arithmetic  59.2 us (15%)
  blocking collectives  52 us (13%)
  matrix products  29.6 us (7%)
  between operations  13.7 us (3%)
  starting transfers between devices  9.79 us (2%)
    slice x24, local copies, waits for them, and re-layouts, channel_conv(): _, states = lax.associative_scan(combine, (decays, closing), axis=0)  83.2 us
    all_gather x1, waiting for transfers between devices, shards(): lax.all_gather(gated_mix, 'ch', axis=1, tiled=True)  57.5 us
    all_to_all x1, blocking collectives, shards(): lax.all_to_all(long_part, 'ctx', split_axis=1, concat_axis=0, tiled=True)  52 us
    unnamed x26, local copies, waits for them, and re-layouts  27.2 us
    all_to_all x1, waiting for transfers between devices, shards(): lax.all_to_all(channel_major, 'ctx', split_axis=0, concat_axis=1, tiled=T...  26.5 us
    add x1, other arithmetic, shards(): featured + tap_weights[tap_index].astype(jnp.float32)[:, None, :] * exten...  15.7 us
    gather x2, local copies, waits for them, and re-layouts, make_tables(): kernel[jnp.maximum(offsets, 0)]  15.3 us
    dot_general x1, matrix products, shards(): jnp.dot(lax.all_gather(gated_mix, 'ch', axis=1, tiled=True), out_weight,...  14.7 us
  transfers between devices with their start and end apart: 3, of which 2 were waited for; matrix products, arithmetic and copies ran while one was open for 8% of the time, Pallas kernels for 0%

commit v1 on v0

--- a/solution.py
+++ b/solution.py
@@ -1,9 +1,29 @@
+import functools
 import jax
 import jax.numpy as jnp
 from jax import lax
 from jax.sharding import PartitionSpec as P
 
 BLOCK = 64
+
+
+def proceed_bars(row_data, net_axis, along_dim, out_dim):
+    carry, finding = (lax.psum(1, net_axis), lax.axis_index(net_axis))
+    local_part = row_data.shape[along_dim] // carry
+    spare = jnp.roll(row_data, -finding * local_part, along_dim)
+    crops = [lax.slice_in_dim(spare, 0, local_part, axis=along_dim)]
+    for dev in range(1, carry):
+        shaped = lax.slice_in_dim(spare, dev * local_part, (dev + 1) * local_part, axis=along_dim)
+        crops.append(
+            lax.ppermute(shaped, net_axis, [(num, (num + dev) % carry) for num in range(carry)])
+        )
+    work_now = jnp.roll(
+        jnp.concatenate(crops[::-1], out_dim), (finding + 1) * crops[0].shape[out_dim], out_dim
+    )
+    return work_now
+
+
+switch_tiles = functools.partial(proceed_bars, net_axis="ctx", along_dim=1, out_dim=0)
 
 
 def shifted(value, axis, steps):
@@ -73,7 +93,7 @@
     rates_here = lax.dynamic_slice_in_dim(pole_rates, first_channel, share_width, 1)
     residues_here = lax.dynamic_slice_in_dim(residues, first_channel, share_width, 1)
     long_part = channel_conv(spread, rates_here, residues_here).astype(jnp.bfloat16)
-    returned = lax.all_to_all(long_part, "ctx", split_axis=1, concat_axis=0, tiled=True)
+    returned = switch_tiles(long_part)
     long_mix = jnp.transpose(returned)
     gated_mix = featured[0] * (
         long_mix.astype(jnp.float32) + long_bias[None, :] * mixed_input.astype(jnp.float32)

time: 408 us -> 405 us (level)
  blocking collectives: 52 us -> 0 us
  waiting for transfers between devices: 84 us -> 126 us
  starting transfers between devices: 9.79 us -> 17.5 us
    all_to_all x1 -> x0, blocking collectives: 52 us -> none  [shards(): lax.all_to_all(long_part, 'ctx', split_axis=1, concat_axis=0, tiled=True)]
    ppermute x0 -> x7, waiting for transfers between devices: none -> 40 us  [proceed_bars(): lax.ppermute(shaped, net_axis, [(num, (num + dev) % carry) for num in ran...]
    ppermute x0 -> x7, starting transfers between devices: none -> 7.68 us  [proceed_bars(): lax.ppermute(shaped, net_axis, [(num, (num + dev) % carry) for num in ran...]
    convert_element_type x1 -> x0, local copies, waits for them, and re-layouts: 5.36 us -> none  [shards(): long_mix.astype(jnp.float32)]
    convert_element_type x1 -> x2, local copies, waits for them, and re-layouts: 3.29 us -> 7.4 us  [shards(): channel_conv(spread, rates_here, residues_here).astype(jnp.bfloat16)]
    unnamed x26 -> x41, local copies, waits for them, and re-layouts: 27.2 us -> 27.4 us
  transfers between devices with their start and end apart: 3 -> 10, of which waited for: 2 -> 7; matrix products, arithmetic and copies ran while one was open for 8% -> 8% of each run, Pallas kernels for 0% -> 0%
where the time goes in v1:
time: 405 us; the launch traced here: 402 us
  local copies, waits for them, and re-layouts  157 us (39%)
  waiting for transfers between devices  126 us (31%)
  other arithmetic  58.5 us (14%)
  matrix products  29.6 us (7%)
  starting transfers between devices  17.5 us (4%)
  between operations  13.9 us (3%)
    slice x24, local copies, waits for them, and re-layouts, channel_conv(): _, states = lax.associative_scan(combine, (decays, closing), axis=0)  83.2 us
    all_gather x1, waiting for transfers between devices, shards(): lax.all_gather(gated_mix, 'ch', axis=1, tiled=True)  59.4 us
    ppermute x7, waiting for transfers between devices, proceed_bars(): lax.ppermute(shaped, net_axis, [(num, (num + dev) % carry) for num in ran...  40 us
    unnamed x41, local copies, waits for them, and re-layouts  27.4 us
    all_to_all x1, waiting for transfers between devices, shards(): lax.all_to_all(channel_major, 'ctx', split_axis=0, concat_axis=1, tiled=T...  26.5 us
    add x1, other arithmetic, shards(): featured + tap_weights[tap_index].astype(jnp.float32)[:, None, :] * exten...  15.7 us
    gather x2, local copies, waits for them, and re-layouts, make_tables(): kernel[jnp.maximum(offsets, 0)]  15.3 us
    dot_general x1, matrix products, shards(): jnp.dot(lax.all_gather(gated_mix, 'ch', axis=1, tiled=True), out_weight,...  14.7 us
  transfers between devices with their start and end apart: 10, of which 7 were waited for; matrix products, arithmetic and copies ran while one was open for 8% of the time, Pallas kernels for 0%

profile of v1, /device:TPU:0, one launch (start us, length us, event | category | flops | bytes accessed | tf_op | source)
XLA Modules:
  0.0 402.4 jit_solution(9385975646173363368)
XLA Ops:
  7.4 4.9 %collective-permute-start = (bf16[3,2,1024]{2,1,0:T(2,128)(2,1)S(1)}, bf16[3,2,1024]{2,1,0:T(2,128)(2,1)S(1)}, u32[]{:S(2)}, u32[]{:S(2)}) collective-permute-start(bf16[3,2,1024]{2,1,0:T(2,128)(2,1)S(1)} %slice.200), channel_id=1, source_target_pairs={{0,4},{4,8},{8,12},{12,16},{16,20},{20,24},{24,28},{1,5},{5,9},{9,... | collective-permute-start | bytes 36872 | tf_op jit(solution)/shard_map/ppermute | solution.py:32
  13.0 8.6 %copy.44 = bf16[3,1024,1024]{1,2,0:T(8,128)(2,1)} copy(bf16[3,1024,1024]{2,1,0:T(8,128)(2,1)} %param.6) | data formatting | bytes 12582912 | tf_op args[0]
  22.0 15.7 %multiply_add_fusion = f32[3,1024,1024]{1,2,0:T(8,128)S(1)} fusion(bf16[3,1024,1024]{1,2,0:T(8,128)(2,1)} %copy.44, bf16[3,2,1024]{1,2,0:T(8,128)(2,1)S(1)} %copy.45, f32[3,1024]{1,0:T(4,128)S(1)} %get-tuple-element.19, f32[3,1024]{1,0:T(4,128)S(1)} %get-tuple-element.20, f32[3,1024]{1,0:T(4,128)S(1)} %get-tuple-element.18), kind=kLoop, calls=%fused_computation.1 | loop fusion | flops 44040192 | bytes 18923520 | tf_op jit(solution)/shard_map/add | solution.py:85
  37.8 4.5 %copy-done = f32[3,1024,1024]{1,2,0:T(8,128)} copy-done((f32[3,1024,1024]{1,2,0:T(8,128)}, f32[3,1024,1024]{1,2,0:T(8,128)S(1)}, u32[]{:S(2)}) %copy-start) | copy-done | bytes 12582936
  44.3 4.9 %all-to-all-start = ((bf16[8,128,1024]{2,1,0:T(8,128)(2,1)}), bf16[8,128,1024]{2,1,0:T(8,128)(2,1)}, u32[]{:S(2)}, u32[]{:S(2)}) async-start(bf16[8,128,1024]{2,1,0:T(8,128)(2,1)} %bitcast.6), calls=%async_computation | async-start | bytes 4194304 | tf_op jit(solution)/shard_map/all_to_all | solution.py:90
  53.5 10.8 %gather_fusion = f32[4096,128]{1,0:T(8,128)S(1)} fusion(f32[64,128]{1,0:T(8,128)S(1)} %copy.50, s32[4096]{0:T(1024)S(1)} %broadcast_clamp_fusion), kind=kCustom, calls=%fused_computation | custom fusion | bytes 4210688 | tf_op jit(solution)/shard_map/gather | solution.py:44
  64.3 4.6 %copy.51 = f32[64,64,128]{1,0,2:T(8,128)} copy(f32[64,64,128]{2,1,0:T(8,128)S(1)} %bitcast.52) | data formatting | bytes 4194304 | tf_op jit(solution)/shard_map/gather | solution.py:44
  70.8 26.5 %all-to-all-done = bf16[8,128,1024]{2,1,0:T(8,128)(2,1)} async-done(((bf16[8,128,1024]{2,1,0:T(8,128)(2,1)}), bf16[8,128,1024]{2,1,0:T(8,128)(2,1)}, u32[]{:S(2)}, u32[]{:S(2)}) %all-to-all-start) | async-done | bytes 2097184 | tf_op jit(solution)/shard_map/all_to_all | solution.py:90
  97.3 3.9 copy.47
  101.2 3.8 copy.52
  108.0 20.3 %slice.211 = f32[64,2048]{0,1:T(8,128)} slice(f32[128,2048]{0,1:T(8,128)S(1)} %bitcast.48), slice={[0:127:2], [0:2048:1]} | slice | bytes 1048576 | tf_op jit(solution)/shard_map/slice | solution.py:70
  128.2 21.9 %slice.212 = f32[64,2048]{0,1:T(8,128)} slice(f32[128,2048]{0,1:T(8,128)S(1)} %bitcast.49), slice={[1:128:2], [0:2048:1]} | slice | bytes 1048576 | tf_op jit(solution)/shard_map/slice | solution.py:70
  184.4 21.6 %slice.250 = f32[63,2048]{0,1:T(8,128)} slice(f32[128,2048]{0,1:T(8,128)S(1)} %bitcast.50), slice={[2:128:2], [0:2048:1]} | slice | bytes 1032192 | tf_op jit(solution)/shard_map/slice | solution.py:70
  225.5 4.6 %pad.124 = f32[128,2048]{1,0:T(8,128)} pad(f32[64,2048]{1,0:T(8,128)} %add.150, f32[]{:T(128)} %constant.53.clone.1), padding=1_0_1x0_0_0 | pad | bytes 1572868
  243.5 4.2 %fusion.4 = f32[128,128,64]{1,2,0:T(8,128)S(1)} fusion(bf16[128,128,64]{1,2,0:T(8,128)(2,1)S(1)} %copy.52, f32[64,64,128]{1,0,2:T(8,128)} %copy.51, pred[64,64]{1,0:T(8,128)(4,1)S(1)} %copy-done.8), kind=kOutput, calls=%fused_computation.14 | convolution fusion | flops 805830656 | bytes 8392704 | tf_op jit(solution)/shard_map/cij,cnj->cni/dot_general | solution.py:65
  247.7 7.8 %add_convert_fusion = bf16[128,128,64]{1,2,0:T(8,128)(2,1)S(1)} fusion(f32[128,128,64]{1,2,0:T(8,128)S(1)} %fusion.4, f32[128,128,16]{0,2,1:T(8,128)S(1)} %bitcast.55, f32[16,128]{0,1:T(8,128)S(1)} %copy-done.6, f32[16,128]{0,1:T(8,128)S(1)} %copy-done.5, f32[16,128]{0,1:T(8,128)S(1)} %copy-done.3), kind=kOutput, calls=%fused_computation.16 | convolution fusion | flops 203816960 | bytes 7364608 | tf_op jit(solution)/shard_map/ipc,ncp->cni/dot_general | solution.py:73
  258.8 4.1 %copy.62 = bf16[128,8192]{1,0:T(8,128)(2,1)} copy(bf16[128,8192]{0,1:T(8,128)(2,1)} %bitcast.54) | data formatting | bytes 4194304 | tf_op jit(solution)/shard_map/convert_element_type | solution.py:95
  268.7 4.3 %collective-permute-start.4 = (bf16[128,1024]{1,0:T(8,128)(2,1)}, bf16[128,1024]{1,0:T(8,128)(2,1)S(1)}, u32[]{:S(2)}, u32[]{:S(2)}) collective-permute-start(bf16[128,1024]{1,0:T(8,128)(2,1)} %get-tuple-element.10), channel_id=1, source_target_pairs={{0,16},{4,20},{8,24},{12,28},{16,0},{20,4},{24,8},{28,12},{1,17},{... | collective-permute-start | bytes 786440 | tf_op jit(solution)/shard_map/ppermute | solution.py:18
  276.3 5.7 %collective-permute-done.2 = bf16[128,1024]{1,0:T(8,128)(2,1)S(1)} collective-permute-done((bf16[128,1024]{1,0:T(8,128)(2,1)}, bf16[128,1024]{1,0:T(8,128)(2,1)S(1)}, u32[]{:S(2)}, u32[]{:S(2)}) %collective-permute-start.2) | collective-permute-done | bytes 262176 | tf_op jit(solution)/shard_map/ppermute | solution.py:18
  282.0 5.1 %collective-permute-done.3 = bf16[128,1024]{1,0:T(8,128)(2,1)S(1)} collective-permute-done((bf16[128,1024]{1,0:T(8,128)(2,1)}, bf16[128,1024]{1,0:T(8,128)(2,1)S(1)}, u32[]{:S(2)}, u32[]{:S(2)}) %collective-permute-start.3) | collective-permute-done | bytes 262176 | tf_op jit(solution)/shard_map/ppermute | solution.py:18
  287.1 25.9 %collective-permute-done.4 = bf16[128,1024]{1,0:T(8,128)(2,1)S(1)} collective-permute-done((bf16[128,1024]{1,0:T(8,128)(2,1)}, bf16[128,1024]{1,0:T(8,128)(2,1)S(1)}, u32[]{:S(2)}, u32[]{:S(2)}) %collective-permute-start.4) | collective-permute-done | bytes 262176 | tf_op jit(solution)/shard_map/ppermute | solution.py:18
  314.5 6.9 %fusion.3 = bf16[1024,1024]{0,1:T(8,128)(2,1)} fusion(f32[3,1024,1024]{1,2,0:T(8,128)} %copy-done, f32[1024]{0:T(1024)S(1)} %copy-done.9, bf16[2048,1024]{1,0:T(8,128)(2,1)S(1)} %slice_dynamic-update-slice_fusion.1, s32[]{:T(128)S(6)} %select_n.42), kind=kLoop, calls=%fused_computation.10 | loop fusion | flops 8388608 | bytes 16781316 | tf_op jit(solution)/shard_map/convert_element_type | solution.py:101
  321.4 59.4 %all-gather.2.cloned.1.call-done = bf16[1024,4096]{0,1:T(8,128)(2,1)} async-done(((bf16[1024,1024]{0,1:T(8,128)(2,1)}), bf16[1024,4096]{0,1:T(8,128)(2,1)}) %all-gather.2.cloned.1.call-update) | async-done | bytes 8388624 | tf_op jit(solution)/shard_map/all_gather | solution.py:103
  380.8 14.7 %convolution_convert_fusion = bf16[1024,1024]{1,0:T(8,128)(2,1)} fusion(bf16[1024,4096]{0,1:T(8,128)(2,1)} %all-gather.2.cloned.1.call-done, bf16[4096,1024]{1,0:T(8,128)(2,1)} %param.11), kind=kOutput, calls=%fused_computation.21 | convolution fusion | flops 8590983168 | bytes 18874368 | tf_op jit(solution)/shard_map/dot_general | solution.py:102
  (137 shorter events, 93.8 us)
Async XLA Ops:
  7.4 14.2 %collective-permute-start = (bf16[3,2,1024]{2,1,0:T(2,128)(2,1)S(1)}, bf16[3,2,1024]{2,1,0:T(2,128)(2,1)S(1)}, u32[]{:S(2)}, u32[]{:S(2)}) collective-permute-start(bf16[3,2,1024]{2,1,0:T(2,128)(2,1)S(1)} %slice.200), channel_id=1, source_target_pairs={{0,4},{4,8},{8,12},{12,16},{16,20},{20,24},{24,28},{1,5},{5,9},{9,... | collective-permute-start | bytes 36872 | tf_op jit(solution)/shard_map/ppermute | solution.py:32
  37.8 4.5 %copy-start = (f32[3,1024,1024]{1,2,0:T(8,128)}, f32[3,1024,1024]{1,2,0:T(8,128)S(1)}, u32[]{:S(2)}) copy-start(f32[3,1024,1024]{1,2,0:T(8,128)S(1)} %multiply_add_fusion) | copy-start | bytes 37748740
  44.3 52.9 %all-to-all-start = ((bf16[8,128,1024]{2,1,0:T(8,128)(2,1)}), bf16[8,128,1024]{2,1,0:T(8,128)(2,1)}, u32[]{:S(2)}, u32[]{:S(2)}) async-start(bf16[8,128,1024]{2,1,0:T(8,128)(2,1)} %bitcast.6), calls=%async_computation | async-start | bytes 4194304 | tf_op jit(solution)/shard_map/all_to_all | solution.py:90
  49.2 331.6 %all-gather.2.cloned.1.call-start = ((), (), s32[]{:S(2)}) async-start(), calls=%async_computation.1 | async-start | bytes 10485760 | tf_op jit(solution)/shard_map/all_gather | solution.py:103
  50.1 3.4 copy-start.2
  50.2 3.3 copy-start.4
  70.8 89.5 %copy-start.7 = (f32[2048]{0:T(1024)}, f32[2048]{0:T(1024)S(1)}, u32[]{:S(2)}) copy-start(f32[2048]{0:T(1024)S(1)} %get-tuple-element.24) | copy-start | bytes 24580
  181.4 37.7 %slice-start = ((f32[64,2048]{1,0:T(8,128)}), f32[1,2048]{1,0:T(1,128)S(1)}, s32[]{:S(2)}) async-start(f32[64,2048]{1,0:T(8,128)} %multiply_add_fusion.1), calls=%async_computation.2 | async-start | bytes 16384 | tf_op jit(solution)/shard_map/slice | solution.py:70
  210.8 0.7 copy-start.1
  237.1 6.3 %copy-start.8 = (pred[64,64]{1,0:T(8,128)(4,1)S(1)}, pred[64,64]{1,0:T(8,128)(4,1)}, u32[]{:S(2)}) copy-start(pred[64,64]{1,0:T(8,128)(4,1)} %subtract_compare_fusion) | copy-start | bytes 12292
  243.4 4.2 %copy-start.3 = (f32[16,128]{0,1:T(8,128)S(1)}, f32[16,128]{0,1:T(8,128)}, u32[]{:S(2)}) copy-start(f32[16,128]{0,1:T(8,128)} %copy-done.2) | copy-start | bytes 24580
  243.5 4.2 %copy-start.5 = (f32[16,128]{0,1:T(8,128)S(1)}, f32[16,128]{0,1:T(8,128)}, u32[]{:S(2)}) copy-start(f32[16,128]{0,1:T(8,128)} %copy-done.4) | copy-start | bytes 24580
  243.5 4.2 %copy-start.6 = (f32[16,128]{0,1:T(8,128)S(1)}, f32[16,128]{0,1:T(8,128)}, u32[]{:S(2)}) copy-start(f32[16,128]{0,1:T(8,128)} %copy.60) | copy-start | bytes 24580
  266.4 9.5 %collective-permute-start.1 = (bf16[128,1024]{1,0:T(8,128)(2,1)}, bf16[128,1024]{1,0:T(8,128)(2,1)S(1)}, u32[]{:S(2)}, u32[]{:S(2)}) collective-permute-start(bf16[128,1024]{1,0:T(8,128)(2,1)} %get-tuple-element.13), channel_id=1, source_target_pairs={{0,28},{4,0},{8,4},{12,8},{16,12},{20,16},{24,20},{28,24},{1,29},{... | collective-permute-start | bytes 786440 | tf_op jit(solution)/shard_map/ppermute | solution.py:18
  268.7 13.2 %collective-permute-start.2 = (bf16[128,1024]{1,0:T(8,128)(2,1)}, bf16[128,1024]{1,0:T(8,128)(2,1)S(1)}, u32[]{:S(2)}, u32[]{:S(2)}) collective-permute-start(bf16[128,1024]{1,0:T(8,128)(2,1)} %get-tuple-element.12), channel_id=1, source_target_pairs={{0,24},{4,28},{8,0},{12,4},{16,8},{20,12},{24,16},{28,20},{1,25},{... | collective-permute-start | bytes 786440 | tf_op jit(solution)/shard_map/ppermute | solution.py:18
  268.7 18.4 %collective-permute-start.3 = (bf16[128,1024]{1,0:T(8,128)(2,1)}, bf16[128,1024]{1,0:T(8,128)(2,1)S(1)}, u32[]{:S(2)}, u32[]{:S(2)}) collective-permute-start(bf16[128,1024]{1,0:T(8,128)(2,1)} %get-tuple-element.11), channel_id=1, source_target_pairs={{0,20},{4,24},{8,28},{12,0},{16,4},{20,8},{24,12},{28,16},{1,21},{... | collective-permute-start | bytes 786440 | tf_op jit(solution)/shard_map/ppermute | solution.py:18
  268.7 44.3 %collective-permute-start.4 = (bf16[128,1024]{1,0:T(8,128)(2,1)}, bf16[128,1024]{1,0:T(8,128)(2,1)S(1)}, u32[]{:S(2)}, u32[]{:S(2)}) collective-permute-start(bf16[128,1024]{1,0:T(8,128)(2,1)} %get-tuple-element.10), channel_id=1, source_target_pairs={{0,16},{4,20},{8,24},{12,28},{16,0},{20,4},{24,8},{28,12},{1,17},{... | collective-permute-start | bytes 786440 | tf_op jit(solution)/shard_map/ppermute | solution.py:18
  273.0 41.1 %collective-permute-start.5 = (bf16[128,1024]{1,0:T(8,128)(2,1)}, bf16[128,1024]{1,0:T(8,128)(2,1)S(1)}, u32[]{:S(2)}, u32[]{:S(2)}) collective-permute-start(bf16[128,1024]{1,0:T(8,128)(2,1)} %get-tuple-element.9), channel_id=1, source_target_pairs={{0,12},{4,16},{8,20},{12,24},{16,28},{20,0},{24,4},{28,8},{1,13},{... | collective-permute-start | bytes 786440 | tf_op jit(solution)/shard_map/ppermute | solution.py:18
  275.8 38.7 %copy-start.9 = (f32[1024]{0:T(1024)S(1)}, f32[1024]{0:T(1024)}, u32[]{:S(2)}) copy-start(f32[1024]{0:T(1024)} %param.10) | copy-start | bytes 12292
  275.8 38.3 %collective-permute-start.6 = (bf16[128,1024]{1,0:T(8,128)(2,1)S(1)}, bf16[128,1024]{1,0:T(8,128)(2,1)S(1)}, u32[]{:S(2)}, u32[]{:S(2)}) collective-permute-start(bf16[128,1024]{1,0:T(8,128)(2,1)S(1)} %get-tuple-element.8), channel_id=1, source_target_pairs={{0,8},{4,12},{8,16},{12,20},{16,24},{20,28},{24,0},{28,4},{1,9},{5... | collective-permute-start | bytes 786440 | tf_op jit(solution)/shard_map/ppermute | solution.py:18
  282.0 32.2 %collective-permute-start.7 = (bf16[128,1024]{1,0:T(8,128)(2,1)S(1)}, bf16[128,1024]{1,0:T(8,128)(2,1)S(1)}, u32[]{:S(2)}, u32[]{:S(2)}) collective-permute-start(bf16[128,1024]{1,0:T(8,128)(2,1)S(1)} %get-tuple-element.7), channel_id=1, source_target_pairs={{0,4},{4,8},{8,12},{12,16},{16,20},{20,24},{24,28},{28,0},{1,5},{5... | collective-permute-start | bytes 786440 | tf_op jit(solution)/shard_map/ppermute | solution.py:18
Sparse Core Ops, SparseCore 0:
  321.5 59.2 all-gather.1
